TPU v7x, 512 devices: a whole 4x4x16 slice. The times are simulated.
512 devices in a mesh: dp: 32 (over y, z_lo, core), ctx: 16 (over x, z_hi).
Axes of the slice: x: 4, y: 4, z: 16 (z_hi: 4, z_lo: 4; z = z_hi * 4 + z_lo), core: 2. Of those that a mesh axis runs over, the one named last changes fastest.
Arguments:
- branch_in: bfloat16 [32, 2048, 2816], P('dp', 'ctx'), may hold values from -6 to 6
- cotangent: bfloat16 [32, 2048, 2816], P('dp', 'ctx'), may hold values from -6 to 6
- weight_a: bfloat16 [256, 2816], P('dp', 'ctx'), may hold values from -0.375 to 0.375
- weight_x: bfloat16 [256, 2816], P('dp', 'ctx'), may hold values from -0.375 to 0.375
- conv_weight: bfloat16 [4, 2816], P(None, 'ctx'), may hold values from -3 to 3
- conv_bias: bfloat16 [2816], P('ctx'), may hold values from -3 to 3
- bias_a: bfloat16 [2816], P('ctx'), may hold values from -4 to 4
- bias_x: bfloat16 [2816], P('ctx'), may hold values from -4 to 4
- rate: bfloat16 [2816], P('ctx'), may hold values from 0 to 0.016, as said below
Outputs:
- grad_input: bfloat16 [32, 2048, 2816], P('dp', 'ctx')
- grad_weight_a: float32 [256, 2816], P('dp', 'ctx')
- grad_rate: float32 [2816], replicated
Inputs may be any that keep to these rules, and one draw needn't show every extreme that they name: `rate`: positive in every channel.
All inputs are finite; a program needn't handle non-finite values.
Results may differ from a plain program's by a relative error of at most 0.006.
Values may be sent and summed in bfloat16 or wider, within the bound.
No kernel may reach another device: no remote copies, remote signals or barrier semaphores. Data moves between devices by JAX's collectives and lax.ppermute only.
A program may use at most 128 MiB of HBM per device.

v0:
```python
import jax
import jax.numpy as jnp
from jax import lax
from jax.sharding import PartitionSpec as P

floor_value = 2.5e-07
exact = lax.Precision.HIGHEST


def passed_along(array, axis, by):
    length = lax.axis_size(axis)
    pairs = [(i, i + by) for i in range(length) if 0 <= i + by < length]
    return lax.ppermute(array, axis, pairs)


def mix_heads(values, weights):
    tokens = values.shape[0]
    head_width = weights.shape[0]
    head_count = weights.shape[1] // head_width
    left = values.reshape(tokens, head_count, head_width)
    right = weights.reshape(head_width, head_count, head_width)
    result = jnp.einsum("thk,khj->thj", left, right, preferred_element_type=jnp.float32)
    return result.reshape(tokens, head_count * head_width)


def back_heads(grads, weights):
    tokens = grads.shape[0]
    head_width = weights.shape[0]
    head_count = weights.shape[1] // head_width
    left = grads.reshape(tokens, head_count, head_width)
    right = weights.reshape(head_width, head_count, head_width)
    result = jnp.einsum("thj,khj->thk", left, right, preferred_element_type=jnp.float32)
    return result.reshape(tokens, head_count * head_width)


def grad_heads(values, grads, head_width):
    tokens = values.shape[0]
    head_count = values.shape[1] // head_width
    left = values.reshape(tokens, head_count, head_width)
    right = grads.reshape(tokens, head_count, head_width)
    result = jnp.einsum("thk,thj->khj", left, right, preferred_element_type=jnp.float32)
    return result.reshape(head_width, head_count * head_width)


def compose(own, received):
    return (own[0] * received[0], own[0] * received[1] + own[1])


def block_prefix(forward_item, backward_item, axis):
    span = lax.axis_size(axis)
    ones = jnp.ones_like(forward_item[0])
    zeros = jnp.zeros_like(forward_item[0])
    fwd_incl, fwd_excl = (forward_item, (ones, zeros))
    bwd_incl, bwd_excl = (backward_item, (ones, zeros))
    shift = 1
    while shift < span:
        got_fwd = passed_along(jnp.stack(fwd_incl), axis, shift)
        got_bwd = passed_along(jnp.stack(bwd_incl), axis, -shift)
        got_fwd = (got_fwd[0], got_fwd[1])
        got_bwd = (got_bwd[0], got_bwd[1])
        fwd_excl = compose(fwd_excl, got_fwd)
        fwd_incl = compose(fwd_incl, got_fwd)
        bwd_excl = compose(bwd_excl, got_bwd)
        bwd_incl = compose(bwd_incl, got_bwd)
        shift *= 2
    return (fwd_excl[1], bwd_excl[1])


def summed_apart(parts, shared, axis):
    count, size = parts.shape
    stacked = jnp.concatenate([parts, jnp.broadcast_to(shared[None], (count, shared.shape[0]))], 1)
    sublanes = 8
    total = stacked.shape[1]
    tile = sublanes * 256
    padded = -(-total // tile) * tile
    stacked = jnp.pad(stacked, ((0, 0), (0, padded - total)))
    stacked = stacked.reshape(count * sublanes, padded // sublanes)
    mine = lax.psum_scatter(stacked, axis, scatter_dimension=0, tiled=True).reshape(-1)
    return (mine[:size], mine[size:total])


def on_device(
    branch_in, cotangent, weight_a, weight_x, conv_weight, conv_bias, bias_a, bias_x, rate
):
    inputs = branch_in[0]
    upstream = cotangent[0].astype(jnp.float32)
    length = inputs.shape[0]
    taps = conv_weight.shape[0]
    rows, cols = weight_a.shape
    dp_size = lax.axis_size("dp")
    ctx_size = lax.axis_size("ctx")
    packed = jnp.concatenate(
        [conv_weight, conv_bias[None], bias_a[None], bias_x[None], rate[None]], 0
    )
    both = lax.all_gather(jnp.concatenate([weight_a, weight_x], 0), "dp", axis=0, tiled=True)
    both = both.reshape(dp_size, 2, rows, cols).transpose(1, 0, 2, 3)
    head_width = dp_size * rows
    joined = jnp.concatenate([both.reshape(2 * head_width, cols), packed], 0)
    joined = lax.all_gather(joined, "ctx", axis=0, tiled=True)
    joined = joined.reshape(ctx_size, -1, cols).transpose(1, 0, 2).reshape(-1, ctx_size * cols)
    full_a = joined[:head_width]
    full_x = joined[head_width : 2 * head_width]
    params = joined[2 * head_width :]
    params = params.astype(jnp.float32)
    taps_f = params[:taps]
    cbias = params[taps]
    abias = params[taps + 1]
    xbias = params[taps + 2]
    rates = params[taps + 3]
    width = params.shape[1]
    tail = passed_along(inputs[length - (taps - 1) :], "ctx", 1)
    padded = jnp.concatenate([tail, inputs], 0).astype(jnp.float32)
    conv = cbias
    for tap in range(taps):
        conv = conv + taps_f[tap] * padded[tap : tap + length]
    conv_b = conv.astype(jnp.bfloat16)
    conv_f = conv_b.astype(jnp.float32)
    recur_gate = jax.nn.sigmoid(mix_heads(conv_b, full_a) + abias)
    input_gate = jax.nn.sigmoid(mix_heads(conv_b, full_x) + xbias)
    log_decay = -8.0 * recur_gate * rates
    decay = jnp.exp(log_decay)
    one_minus = -jnp.expm1(2.0 * log_decay)
    multiplier = jnp.sqrt(jnp.maximum(one_minus, floor_value))
    drive = multiplier * input_gate * conv_f
    row_id = lax.broadcasted_iota(jnp.int32, (length, length), 0)
    col_id = lax.broadcasted_iota(jnp.int32, (length, length), 1)
    lower = (row_id >= col_id).astype(jnp.float32)
    upper = (row_id <= col_id).astype(jnp.float32)
    cum_log = jnp.dot(lower, log_decay, precision=exact)
    grow = jnp.exp(cum_log)
    shrink = jnp.exp(-cum_log)
    local_hidden = grow * jnp.dot(lower, shrink * drive, precision=exact)
    weighted_back = jnp.dot(upper, grow * upstream, precision=exact)
    local_back = shrink * weighted_back
    block_decay = grow[-1]
    state_in, back_in = block_prefix(
        (block_decay, local_hidden[-1]), (block_decay, weighted_back[0]), "ctx"
    )
    hidden = local_hidden + grow * state_in
    previous = jnp.concatenate([state_in[None], hidden[:-1]], 0)
    back = local_back + block_decay * shrink * back_in
    slope = jnp.where(one_minus > floor_value, 0.5 / multiplier, 0.0)
    d_mult = back * input_gate * conv_f
    d_log = back * previous * decay - 2.0 * decay * decay * d_mult * slope
    d_recur = (d_log * (-8.0 * rates) * recur_gate * (1.0 - recur_gate)).astype(jnp.bfloat16)
    d_input = (back * multiplier * conv_f * input_gate * (1.0 - input_gate)).astype(jnp.bfloat16)
    d_conv = (
        back * multiplier * input_gate + back_heads(d_recur, full_a) + back_heads(d_input, full_x)
    )
    following = passed_along(d_conv[: taps - 1], "ctx", -1)
    dpad = jnp.concatenate([d_conv, following], 0)
    grad_in = jnp.zeros((length, width), jnp.float32)
    for tap in range(taps):
        start = taps - 1 - tap
        grad_in = grad_in + taps_f[tap] * dpad[start : start + length]
    local_wgrad = grad_heads(conv_b, d_recur, head_width)
    local_rgrad = jnp.sum(d_log * (-8.0 * recur_gate), axis=0)
    by_channel = local_wgrad.reshape(head_width, ctx_size, cols).transpose(1, 0, 2)
    channel_sum, rgrad = summed_apart(by_channel.reshape(ctx_size, -1), local_rgrad, "ctx")
    by_row = channel_sum.reshape(dp_size, rows * cols)
    row_sum, rgrad = summed_apart(by_row, rgrad, "dp")
    wgrad = row_sum.reshape(rows, cols)
    return (grad_in.astype(jnp.bfloat16)[None], wgrad, rgrad)


def solution(mesh):
    placed = (
        P("dp", "ctx", None),
        P("dp", "ctx", None),
        P("dp", "ctx"),
        P("dp", "ctx"),
        P(None, "ctx"),
        P("ctx"),
        P("ctx"),
        P("ctx"),
        P("ctx"),
    )
    return jax.shard_map(
        on_device,
        mesh=mesh,
        in_specs=placed,
        out_specs=(P("dp", "ctx", None), P("dp", "ctx"), P()),
        check_vma=False,
    )
```

profile of v0, /device:TPU:2, one launch (start us, length us, event | category | flops | bytes accessed | tf_op | source)
XLA Modules:
  0.0 590.4 jit_solution(10837949532559104495)
XLA Ops:
  10.6 45.6 %all_gather.6 = bf16[512,176]{1,0:T(8,128)(2,1)S(1)} all-gather(bf16[16,176]{1,0:T(8,128)(2,1)S(1)} %pad_maximum_fusion.11), channel_id=1, replica_groups=mesh['dp'=32,'ctx'=16] {'dp'}, dimensions={0}, use_global_device_ids=true | all-gather | bytes 185856 | tf_op jit(solution)/shard_map/all_gather | solution.py:95
  58.0 9.1 %collective-permute-start = (bf16[3,2816]{1,0:T(4,128)(2,1)S(1)}, bf16[3,2816]{1,0:T(4,128)(2,1)S(1)}, u32[]{:S(2)}, u32[]{:S(2)}) collective-permute-start(bf16[3,2816]{1,0:T(4,128)(2,1)S(1)} %slice_bitcast_fusion), channel_id=1, source_target_pairs={{0,1},{1,2},{2,3},{3,4},{4,5},{5,6},{6,7},{7,8},{8,9},{9,10},{10,1... | collective-permute-start | bytes 50696 | tf_op jit(solution)/shard_map/ppermute | solution.py:13
  70.1 109.5 %all-gather.3.cloned.1.call-done = bf16[16,520,176]{1,2,0:T(8,128)(2,1)} async-done(((bf16[1,520,176]{1,2,0:T(8,128)(2,1)}), bf16[16,520,176]{1,2,0:T(8,128)(2,1)}) %all-gather.3.cloned.1.call-update) | async-done | bytes 2928656 | tf_op jit(solution)/shard_map/all_gather | solution.py:99
  180.9 3.1 fusion.45
  184.0 7.0 %slice_reduce_fusion = (f32[16,176]{1,0:T(8,128)S(1)}, f32[16,176]{1,0:T(8,128)S(1)}, f32[16,176]{1,0:T(8,128)S(1)}, f32[16,176]{1,0:T(8,128)S(1)}, f32[16,176]{...) fusion(f32[8,16,176]{0,2,1:T(8,128)S(1)} %slice_convert_fusion), kind=kLoop, calls=%fused_computation.29 | loop fusion | flops 2816 | bytes 180224 | tf_op jit(solution)/shard_map/slice | solution.py:108
  201.2 3.2 fusion.47
  214.4 5.1 collective-permute-start.5
  219.5 5.5 collective-permute-start.1
  225.1 4.1 collective-permute-done.1
  229.2 7.3 %collective-permute-start.6 = (f32[2,2816]{1,0:T(2,128)S(1)}, f32[2,2816]{1,0:T(2,128)S(1)}, u32[]{:S(2)}, u32[]{:S(2)}) collective-permute-start(f32[2,2816]{1,0:T(2,128)S(1)} %pad_maximum_fusion.8), channel_id=1, source_target_pairs={{0,2},{1,3},{2,4},{3,5},{4,6},{5,7},{6,8},{7,9},{8,10},{9,11},{10,... | collective-permute-start | bytes 67592 | tf_op jit(solution)/shard_map/ppermute | solution.py:13
  236.6 8.2 %collective-permute-start.2 = (f32[2,2816]{1,0:T(2,128)S(1)}, f32[2,2816]{1,0:T(2,128)S(1)}, u32[]{:S(2)}, u32[]{:S(2)}) collective-permute-start(f32[2,2816]{1,0:T(2,128)S(1)} %pad_maximum_fusion.5), channel_id=1, source_target_pairs={{2,0},{3,1},{4,2},{5,3},{6,4},{7,5},{8,6},{9,7},{10,8},{11,9},{12,... | collective-permute-start | bytes 67592 | tf_op jit(solution)/shard_map/ppermute | solution.py:13
  244.8 3.4 collective-permute-start.7
  248.2 3.0 collective-permute-done.2
  254.1 3.8 collective-permute-start.8
  259.6 5.6 collective-permute-done.4
  265.3 4.6 multiply_reduce_fusion
  274.9 4.8 copy.60
  279.7 5.8 reshape.115
  289.5 3.4 reshape.116
  297.1 3.0 copy.54
  304.5 127.1 %reduce-scatter.3.cloned.1.call-done = f32[8,6144]{1,0:T(8,128)} async-done(((f32[128,6144]{1,0:T(8,128)}), f32[8,6144]{1,0:T(8,128)}) %reduce-scatter.3.cloned.1.call-update) | async-done | bytes 196624 | tf_op jit(solution)/shard_map/reduce_scatter | solution.py:78
  438.2 5.8 collective-permute-start.9
  444.0 4.0 collective-permute-done.9
  449.5 132.4 %reduce-scatter.5.cloned.1.call-done = f32[8,768]{1,0:T(8,128)} async-done(((f32[256,768]{1,0:T(8,128)}), f32[8,768]{1,0:T(8,128)}) %reduce-scatter.5.cloned.1.call-update) | async-done | bytes 24592 | tf_op jit(solution)/shard_map/reduce_scatter | solution.py:78
  (106 shorter events, 61.7 us)
Async XLA Ops:
  7.2 50.8 %copy-start.9 = (bf16[1,128,2816]{2,1,0:T(8,128)(2,1)S(1)}, bf16[1,128,2816]{2,1,0:T(8,128)(2,1)}, u32[]{:S(2)}) copy-start(bf16[1,128,2816]{2,1,0:T(8,128)(2,1)} %param.9) | copy-start | bytes 2162692
  7.2 172.5 %all-gather.3.cloned.1.call-start = ((), (), s32[]{:S(2)}) async-start(), calls=%async_computation.4 | async-start | bytes 3829760 | tf_op jit(solution)/shard_map/all_gather | solution.py:99
  57.9 373.6 %reduce-scatter.3.cloned.1.call-start = ((), (), s32[]{:S(2)}) async-start(), calls=%async_computation.2 | async-start | bytes 3342336 | tf_op jit(solution)/shard_map/reduce_scatter | solution.py:78
  58.0 11.9 %collective-permute-start = (bf16[3,2816]{1,0:T(4,128)(2,1)S(1)}, bf16[3,2816]{1,0:T(4,128)(2,1)S(1)}, u32[]{:S(2)}, u32[]{:S(2)}) collective-permute-start(bf16[3,2816]{1,0:T(4,128)(2,1)S(1)} %slice_bitcast_fusion), channel_id=1, source_target_pairs={{0,1},{1,2},{2,3},{3,4},{4,5},{5,6},{6,7},{7,8},{8,9},{9,10},{10,1... | collective-permute-start | bytes 50696 | tf_op jit(solution)/shard_map/ppermute | solution.py:13
  207.3 2.8 copy-start.1
  207.3 2.9 copy-start.2
  207.3 2.9 copy-start.8
  210.2 3.0 copy-start.10
  214.4 10.7 %collective-permute-start.5 = (f32[2,2816]{1,0:T(2,128)S(1)}, f32[2,2816]{1,0:T(2,128)S(1)}, u32[]{:S(2)}, u32[]{:S(2)}) collective-permute-start(f32[2,2816]{1,0:T(2,128)S(1)} %get-tuple-element.36), channel_id=1, source_target_pairs={{0,1},{1,2},{2,3},{3,4},{4,5},{5,6},{6,7},{7,8},{8,9},{9,10},{10,1... | collective-permute-start | bytes 67592 | tf_op jit(solution)/shard_map/ppermute | solution.py:13
  219.5 9.6 %collective-permute-start.1 = (f32[2,2816]{1,0:T(2,128)S(1)}, f32[2,2816]{1,0:T(2,128)S(1)}, u32[]{:S(2)}, u32[]{:S(2)}) collective-permute-start(f32[2,2816]{1,0:T(2,128)S(1)} %get-tuple-element.37), channel_id=1, source_target_pairs={{1,0},{2,1},{3,2},{4,3},{5,4},{6,5},{7,6},{8,7},{9,8},{10,9},{11,1... | collective-permute-start | bytes 67592 | tf_op jit(solution)/shard_map/ppermute | solution.py:13
  229.2 15.5 %collective-permute-start.6 = (f32[2,2816]{1,0:T(2,128)S(1)}, f32[2,2816]{1,0:T(2,128)S(1)}, u32[]{:S(2)}, u32[]{:S(2)}) collective-permute-start(f32[2,2816]{1,0:T(2,128)S(1)} %pad_maximum_fusion.8), channel_id=1, source_target_pairs={{0,2},{1,3},{2,4},{3,5},{4,6},{5,7},{6,8},{7,9},{8,10},{9,11},{10,... | collective-permute-start | bytes 67592 | tf_op jit(solution)/shard_map/ppermute | solution.py:13
  236.6 14.6 %collective-permute-start.2 = (f32[2,2816]{1,0:T(2,128)S(1)}, f32[2,2816]{1,0:T(2,128)S(1)}, u32[]{:S(2)}, u32[]{:S(2)}) collective-permute-start(f32[2,2816]{1,0:T(2,128)S(1)} %pad_maximum_fusion.5), channel_id=1, source_target_pairs={{2,0},{3,1},{4,2},{5,3},{6,4},{7,5},{8,6},{9,7},{10,8},{11,9},{12,... | collective-permute-start | bytes 67592 | tf_op jit(solution)/shard_map/ppermute | solution.py:13
  244.8 9.2 %collective-permute-start.7 = (f32[2,2816]{1,0:T(2,128)S(1)}, f32[2,2816]{1,0:T(2,128)S(1)}, u32[]{:S(2)}, u32[]{:S(2)}) collective-permute-start(f32[2,2816]{1,0:T(2,128)S(1)} %pad_maximum_fusion.9), channel_id=1, source_target_pairs={{0,4},{1,5},{2,6},{3,7},{4,8},{5,9},{6,10},{7,11},{8,12},{9,13},{1... | collective-permute-start | bytes 67592 | tf_op jit(solution)/shard_map/ppermute | solution.py:13
  251.3 6.7 %collective-permute-start.3 = (f32[2,2816]{1,0:T(2,128)S(1)}, f32[2,2816]{1,0:T(2,128)S(1)}, u32[]{:S(2)}, u32[]{:S(2)}) collective-permute-start(f32[2,2816]{1,0:T(2,128)S(1)} %pad_maximum_fusion.6), channel_id=1, source_target_pairs={{4,0},{5,1},{6,2},{7,3},{8,4},{9,5},{10,6},{11,7},{12,8},{13,9},{1... | collective-permute-start | bytes 67592 | tf_op jit(solution)/shard_map/ppermute | solution.py:13
  254.1 5.3 collective-permute-start.8
  258.0 7.2 %collective-permute-start.4 = (f32[2,2816]{1,0:T(2,128)S(1)}, f32[2,2816]{1,0:T(2,128)S(1)}, u32[]{:S(2)}, u32[]{:S(2)}) collective-permute-start(f32[2,2816]{1,0:T(2,128)S(1)} %pad_maximum_fusion.7), channel_id=1, source_target_pairs={{8,0},{9,1},{10,2},{11,3},{12,4},{13,5},{14,6},{15,7},{24,16},{25,... | collective-permute-start | bytes 67592 | tf_op jit(solution)/shard_map/ppermute | solution.py:13
  271.2 1.5 copy-start.4
  272.7 2.2 copy-start.5
  292.9 1.4 copy-start
  292.9 289.0 %reduce-scatter.5.cloned.1.call-start = ((), (), s32[]{:S(2)}) async-start(), calls=%async_computation.3 | async-start | bytes 811008 | tf_op jit(solution)/shard_map/reduce_scatter | solution.py:78
  297.1 3.0 copy-start.7
  432.7 3.2 copy-start.6
  433.6 2.3 copy-start.3
  438.2 9.8 %collective-permute-start.9 = (f32[3,2816]{1,0:T(4,128)S(1)}, f32[3,2816]{1,0:T(4,128)S(1)}, u32[]{:S(2)}, u32[]{:S(2)}) collective-permute-start(f32[3,2816]{1,0:T(4,128)S(1)} %slice.226), channel_id=1, source_target_pairs={{1,0},{2,1},{3,2},{4,3},{5,4},{6,5},{7,6},{8,7},{9,8},{10,9},{11,1... | collective-permute-start | bytes 101384 | tf_op jit(solution)/shard_map/ppermute | solution.py:13
Sparse Core Ops, SparseCore 0:
  58.1 121.5 all-gather.2
  293.0 138.5 reduce-scatter.2
  436.0 145.7 reduce-scatter.4
where the time goes:
time: 592 us; the launch traced here: 590 us
  waiting for transfers between devices  389 us (66%)
  starting transfers between devices  52.6 us (9%)
  local copies, waits for them, and re-layouts  46.7 us (8%)
  blocking collectives  45.6 us (8%)
  other arithmetic  23.1 us (4%)
  matrix products  19.6 us (3%)
  between operations  14.2 us (2%)
    reduce_scatter x2, waiting for transfers between devices, summed_apart(): lax.psum_scatter(stacked, axis, scatter_dimension=0, tiled=True).reshape(-1)  259 us
    all_gather x1, waiting for transfers between devices, on_device(): joined = lax.all_gather(joined, 'ctx', axis=0, tiled=True)  110 us
    ppermute x10, starting transfers between devices, passed_along(): return lax.ppermute(array, axis, pairs)  52.2 us
    all_gather x1, blocking collectives, on_device(): lax.all_gather(jnp.concatenate([weight_a, weight_x], 0), 'dp', axis=0, ti...  45.6 us
    ppermute x10, waiting for transfers between devices, passed_along(): return lax.ppermute(array, axis, pairs)  19.6 us
  transfers between devices with their start and end apart: 13, of which 9 were waited for; matrix products, arithmetic and copies ran while one was open for 2% of the time, Pallas kernels for 0%

commit v1 on v0

--- a/solution.py
+++ b/solution.py
@@ -2,6 +2,7 @@
 import jax.numpy as jnp
 from jax import lax
 from jax.sharding import PartitionSpec as P
+from jax.lax import all_to_all, axis_size
 
 floor_value = 2.5e-07
 exact = lax.Precision.HIGHEST
@@ -96,7 +97,12 @@
     both = both.reshape(dp_size, 2, rows, cols).transpose(1, 0, 2, 3)
     head_width = dp_size * rows
     joined = jnp.concatenate([both.reshape(2 * head_width, cols), packed], 0)
-    joined = lax.all_gather(joined, "ctx", axis=0, tiled=True)
+    pieces_in = []
+    for _ in range(axis_size("ctx")):
+        pieces_in.append(joined)
+    joined = jnp.concatenate(
+        all_to_all(jnp.stack(pieces_in, 0), axis_name="ctx", split_axis=0, concat_axis=0), 0
+    )
     joined = joined.reshape(ctx_size, -1, cols).transpose(1, 0, 2).reshape(-1, ctx_size * cols)
     full_a = joined[:head_width]
     full_x = joined[head_width : 2 * head_width]

time: 592 us -> 665 us (1.12)
  waiting for transfers between devices: 389 us -> 439 us
  starting transfers between devices: 52.6 us -> 73.9 us
    ppermute x10, waiting for transfers between devices: 19.6 us -> 173 us  [passed_along(): return lax.ppermute(array, axis, pairs)]
    all_gather x1 -> x0, waiting for transfers between devices: 110 us -> none  [on_device(): joined = lax.all_gather(joined, 'ctx', axis=0, tiled=True)]
    all_to_all x0 -> x1, starting transfers between devices: none -> 15.5 us  [on_device(): all_to_all(jnp.stack(pieces_in, 0), axis_name='ctx', split_axis=0, concat...]
where the time goes in v1:
time: 665 us; the launch traced here: 664 us
  waiting for transfers between devices  439 us (66%)
  starting transfers between devices  73.9 us (11%)
  local copies, waits for them, and re-layouts  48.1 us (7%)
  blocking collectives  45.6 us (7%)
  other arithmetic  23.1 us (3%)
  matrix products  19.6 us (3%)
  between operations  14.5 us (2%)
    reduce_scatter x2, waiting for transfers between devices, summed_apart(): lax.psum_scatter(stacked, axis, scatter_dimension=0, tiled=True).reshape(-1)  263 us
    ppermute x10, waiting for transfers between devices, passed_along(): return lax.ppermute(array, axis, pairs)  173 us
    ppermute x10, starting transfers between devices, passed_along(): return lax.ppermute(array, axis, pairs)  58.1 us
    all_gather x1, blocking collectives, on_device(): lax.all_gather(jnp.concatenate([weight_a, weight_x], 0), 'dp', axis=0, ti...  45.6 us
    all_to_all x1, starting transfers between devices, on_device(): all_to_all(jnp.stack(pieces_in, 0), axis_name='ctx', split_axis=0, concat...  15.5 us
  transfers between devices with their start and end apart: 13, of which 9 were waited for; matrix products, arithmetic and copies ran while one was open for 2% of the time, Pallas kernels for 0%

profile of v1, /device:TPU:2, one launch (start us, length us, event | category | flops | bytes accessed | tf_op | source)
XLA Modules:
  0.0 664.2 jit_solution(6726143454927356619)
XLA Ops:
  10.5 45.6 %all_gather.3 = bf16[512,176]{1,0:T(8,128)(2,1)S(1)} all-gather(bf16[16,176]{1,0:T(8,128)(2,1)S(1)} %pad_maximum_fusion.11), channel_id=1, replica_groups=mesh['dp'=32,'ctx'=16] {'dp'}, dimensions={0}, use_global_device_ids=true | all-gather | bytes 185856 | tf_op jit(solution)/shard_map/all_gather | solution.py:96
  59.3 15.5 %all-to-all-start = ((bf16[16,520,176]{1,2,0:T(8,128)(2,1)}), bf16[16,520,176]{1,2,0:T(8,128)(2,1)}, u32[]{:S(2)}, u32[]{:S(2)}) async-start(bf16[16,520,176]{1,2,0:T(8,128)(2,1)} %stack.18), calls=%async_computation | async-start | bytes 7208960 | tf_op jit(solution)/shard_map/all_to_all | solution.py:104
  74.9 7.3 %collective-permute-start = (bf16[3,2816]{1,0:T(4,128)(2,1)S(1)}, bf16[3,2816]{1,0:T(4,128)(2,1)S(1)}, u32[]{:S(2)}, u32[]{:S(2)}) collective-permute-start(bf16[3,2816]{1,0:T(4,128)(2,1)S(1)} %slice_bitcast_fusion), channel_id=1, source_target_pairs={{0,1},{1,2},{2,3},{3,4},{4,5},{5,6},{6,7},{7,8},{8,9},{9,10},{10,1... | collective-permute-start | bytes 50696 | tf_op jit(solution)/shard_map/ppermute | solution.py:14
  82.1 150.9 %collective-permute-done = bf16[3,2816]{1,0:T(4,128)(2,1)S(1)} collective-permute-done((bf16[3,2816]{1,0:T(4,128)(2,1)S(1)}, bf16[3,2816]{1,0:T(4,128)(2,1)S(1)}, u32[]{:S(2)}, u32[]{:S(2)}) %collective-permute-start) | collective-permute-done | bytes 16928 | tf_op jit(solution)/shard_map/ppermute | solution.py:14
  233.2 3.4 all-to-all-done
  237.8 3.1 fusion.45
  240.9 7.0 %slice_reduce_fusion = (f32[16,176]{1,0:T(8,128)S(1)}, f32[16,176]{1,0:T(8,128)S(1)}, f32[16,176]{1,0:T(8,128)S(1)}, f32[16,176]{1,0:T(8,128)S(1)}, f32[16,176]{...) fusion(f32[8,16,176]{0,2,1:T(8,128)S(1)} %slice_convert_fusion), kind=kLoop, calls=%fused_computation.29 | loop fusion | flops 2816 | bytes 180224 | tf_op jit(solution)/shard_map/slice | solution.py:114
  258.1 3.2 fusion.47
  271.3 4.9 collective-permute-start.5
  276.2 16.6 %collective-permute-start.1 = (f32[2,2816]{1,0:T(2,128)S(1)}, f32[2,2816]{1,0:T(2,128)S(1)}, u32[]{:S(2)}, u32[]{:S(2)}) collective-permute-start(f32[2,2816]{1,0:T(2,128)S(1)} %get-tuple-element.37), channel_id=1, source_target_pairs={{1,0},{2,1},{3,2},{4,3},{5,4},{6,5},{7,6},{8,7},{9,8},{10,9},{11,1... | collective-permute-start | bytes 67592 | tf_op jit(solution)/shard_map/ppermute | solution.py:14
  292.8 7.3 %collective-permute-done.1 = f32[2,2816]{1,0:T(2,128)S(1)} collective-permute-done((f32[2,2816]{1,0:T(2,128)S(1)}, f32[2,2816]{1,0:T(2,128)S(1)}, u32[]{:S(2)}, u32[]{:S(2)}) %collective-permute-start.1) | collective-permute-done | bytes 22560 | tf_op jit(solution)/shard_map/ppermute | solution.py:14
  300.2 7.3 %collective-permute-start.6 = (f32[2,2816]{1,0:T(2,128)S(1)}, f32[2,2816]{1,0:T(2,128)S(1)}, u32[]{:S(2)}, u32[]{:S(2)}) collective-permute-start(f32[2,2816]{1,0:T(2,128)S(1)} %pad_maximum_fusion.8), channel_id=1, source_target_pairs={{0,2},{1,3},{2,4},{3,5},{4,6},{5,7},{6,8},{7,9},{8,10},{9,11},{10,... | collective-permute-start | bytes 67592 | tf_op jit(solution)/shard_map/ppermute | solution.py:14
  307.5 8.2 %collective-permute-start.2 = (f32[2,2816]{1,0:T(2,128)S(1)}, f32[2,2816]{1,0:T(2,128)S(1)}, u32[]{:S(2)}, u32[]{:S(2)}) collective-permute-start(f32[2,2816]{1,0:T(2,128)S(1)} %pad_maximum_fusion.5), channel_id=1, source_target_pairs={{2,0},{3,1},{4,2},{5,3},{6,4},{7,5},{8,6},{9,7},{10,8},{11,9},{12,... | collective-permute-start | bytes 67592 | tf_op jit(solution)/shard_map/ppermute | solution.py:14
  317.7 4.2 collective-permute-done.2
  322.0 3.6 collective-permute-start.3
  329.3 5.7 collective-permute-done.4
  335.0 4.6 multiply_reduce_fusion
  344.7 4.8 copy.59
  349.5 5.8 reshape.113
  359.3 3.4 reshape.114
  374.2 130.9 %reduce-scatter.3.cloned.1.call-done = f32[8,6144]{1,0:T(8,128)} async-done(((f32[128,6144]{1,0:T(8,128)}), f32[8,6144]{1,0:T(8,128)}) %reduce-scatter.3.cloned.1.call-update) | async-done | bytes 196624 | tf_op jit(solution)/shard_map/reduce_scatter | solution.py:79
  511.7 5.8 collective-permute-start.9
  517.5 4.0 collective-permute-done.9
  523.0 132.3 %reduce-scatter.5.cloned.1.call-done = f32[8,768]{1,0:T(8,128)} async-done(((f32[256,768]{1,0:T(8,128)}), f32[8,768]{1,0:T(8,128)}) %reduce-scatter.5.cloned.1.call-update) | async-done | bytes 24592 | tf_op jit(solution)/shard_map/reduce_scatter | solution.py:79
  (106 shorter events, 64.4 us)
Async XLA Ops:
  59.2 15.6 %copy-start.9 = (bf16[1,128,2816]{2,1,0:T(8,128)(2,1)S(1)}, bf16[1,128,2816]{2,1,0:T(8,128)(2,1)}, u32[]{:S(2)}) copy-start(bf16[1,128,2816]{2,1,0:T(8,128)(2,1)} %param.9) | copy-start | bytes 2162692
  59.3 177.3 %all-to-all-start = ((bf16[16,520,176]{1,2,0:T(8,128)(2,1)}), bf16[16,520,176]{1,2,0:T(8,128)(2,1)}, u32[]{:S(2)}, u32[]{:S(2)}) async-start(bf16[16,520,176]{1,2,0:T(8,128)(2,1)} %stack.18), calls=%async_computation | async-start | bytes 7208960 | tf_op jit(solution)/shard_map/all_to_all | solution.py:104
  74.8 430.3 %reduce-scatter.3.cloned.1.call-start = ((), (), s32[]{:S(2)}) async-start(), calls=%async_computation.3 | async-start | bytes 3342336 | tf_op jit(solution)/shard_map/reduce_scatter | solution.py:79
  74.9 158.2 %collective-permute-start = (bf16[3,2816]{1,0:T(4,128)(2,1)S(1)}, bf16[3,2816]{1,0:T(4,128)(2,1)S(1)}, u32[]{:S(2)}, u32[]{:S(2)}) collective-permute-start(bf16[3,2816]{1,0:T(4,128)(2,1)S(1)} %slice_bitcast_fusion), channel_id=1, source_target_pairs={{0,1},{1,2},{2,3},{3,4},{4,5},{5,6},{6,7},{7,8},{8,9},{9,10},{10,1... | collective-permute-start | bytes 50696 | tf_op jit(solution)/shard_map/ppermute | solution.py:14
  264.3 2.8 copy-start.1
  264.3 2.9 copy-start.2
  264.3 2.9 copy-start.8
  267.2 3.0 copy-start.10
  271.3 21.5 %collective-permute-start.5 = (f32[2,2816]{1,0:T(2,128)S(1)}, f32[2,2816]{1,0:T(2,128)S(1)}, u32[]{:S(2)}, u32[]{:S(2)}) collective-permute-start(f32[2,2816]{1,0:T(2,128)S(1)} %get-tuple-element.36), channel_id=1, source_target_pairs={{0,1},{1,2},{2,3},{3,4},{4,5},{5,6},{6,7},{7,8},{8,9},{9,10},{10,1... | collective-permute-start | bytes 67592 | tf_op jit(solution)/shard_map/ppermute | solution.py:14
  276.2 23.9 %collective-permute-start.1 = (f32[2,2816]{1,0:T(2,128)S(1)}, f32[2,2816]{1,0:T(2,128)S(1)}, u32[]{:S(2)}, u32[]{:S(2)}) collective-permute-start(f32[2,2816]{1,0:T(2,128)S(1)} %get-tuple-element.37), channel_id=1, source_target_pairs={{1,0},{2,1},{3,2},{4,3},{5,4},{6,5},{7,6},{8,7},{9,8},{10,9},{11,1... | collective-permute-start | bytes 67592 | tf_op jit(solution)/shard_map/ppermute | solution.py:14
  300.2 15.5 %collective-permute-start.6 = (f32[2,2816]{1,0:T(2,128)S(1)}, f32[2,2816]{1,0:T(2,128)S(1)}, u32[]{:S(2)}, u32[]{:S(2)}) collective-permute-start(f32[2,2816]{1,0:T(2,128)S(1)} %pad_maximum_fusion.8), channel_id=1, source_target_pairs={{0,2},{1,3},{2,4},{3,5},{4,6},{5,7},{6,8},{7,9},{8,10},{9,11},{10,... | collective-permute-start | bytes 67592 | tf_op jit(solution)/shard_map/ppermute | solution.py:14
  307.5 14.4 %collective-permute-start.2 = (f32[2,2816]{1,0:T(2,128)S(1)}, f32[2,2816]{1,0:T(2,128)S(1)}, u32[]{:S(2)}, u32[]{:S(2)}) collective-permute-start(f32[2,2816]{1,0:T(2,128)S(1)} %pad_maximum_fusion.5), channel_id=1, source_target_pairs={{2,0},{3,1},{4,2},{5,3},{6,4},{7,5},{8,6},{9,7},{10,8},{11,9},{12,... | collective-permute-start | bytes 67592 | tf_op jit(solution)/shard_map/ppermute | solution.py:14
  315.8 9.8 %collective-permute-start.7 = (f32[2,2816]{1,0:T(2,128)S(1)}, f32[2,2816]{1,0:T(2,128)S(1)}, u32[]{:S(2)}, u32[]{:S(2)}) collective-permute-start(f32[2,2816]{1,0:T(2,128)S(1)} %pad_maximum_fusion.9), channel_id=1, source_target_pairs={{0,4},{1,5},{2,6},{3,7},{4,8},{5,9},{6,10},{7,11},{8,12},{9,13},{1... | collective-permute-start | bytes 67592 | tf_op jit(solution)/shard_map/ppermute | solution.py:14
  322.0 5.7 collective-permute-start.3
  325.7 3.4 collective-permute-start.8
  327.8 7.2 %collective-permute-start.4 = (f32[2,2816]{1,0:T(2,128)S(1)}, f32[2,2816]{1,0:T(2,128)S(1)}, u32[]{:S(2)}, u32[]{:S(2)}) collective-permute-start(f32[2,2816]{1,0:T(2,128)S(1)} %pad_maximum_fusion.7), channel_id=1, source_target_pairs={{8,0},{9,1},{10,2},{11,3},{12,4},{13,5},{14,6},{15,7},{24,16},{25,... | collective-permute-start | bytes 67592 | tf_op jit(solution)/shard_map/ppermute | solution.py:14
  341.0 1.5 copy-start.4
  342.5 2.2 copy-start.5
  362.7 1.4 copy-start
  362.7 292.6 %reduce-scatter.5.cloned.1.call-start = ((), (), s32[]{:S(2)}) async-start(), calls=%async_computation.4 | async-start | bytes 811008 | tf_op jit(solution)/shard_map/reduce_scatter | solution.py:79
  366.8 3.0 copy-start.7
  506.2 3.2 copy-start.6
  507.2 2.3 copy-start.3
  511.7 9.8 %collective-permute-start.9 = (f32[3,2816]{1,0:T(4,128)S(1)}, f32[3,2816]{1,0:T(4,128)S(1)}, u32[]{:S(2)}, u32[]{:S(2)}) collective-permute-start(f32[3,2816]{1,0:T(4,128)S(1)} %slice.226), channel_id=1, source_target_pairs={{1,0},{2,1},{3,2},{4,3},{5,4},{6,5},{7,6},{8,7},{9,8},{10,9},{11,1... | collective-permute-start | bytes 101384 | tf_op jit(solution)/shard_map/ppermute | solution.py:14
Sparse Core Ops, SparseCore 0:
  362.8 142.2 reduce-scatter.2
  509.6 145.7 reduce-scatter.4
